TPU v7x, 256 devices: a whole 4x4x8 slice. The times are simulated.
256 devices in a mesh: dp: 16 (over z, x_lo), own: 16 (over x_hi, y, core).
Axes of the slice: x: 4 (x_hi: 2, x_lo: 2; x = x_hi * 2 + x_lo), y: 4, z: 8, core: 2. Of those that a mesh axis runs over, the one named last changes fastest.
Arguments:
- grads: float32 [16, 16, 1024, 1024], P('dp', None, 'own'), may hold values from -0.27 to 0.27
- owner_map: int32 [16], replicated, may hold values from 0 to 31, as said below
- stat_left: float32 [32, 1024, 1024], P('own', 'dp'), as said below
- stat_right: float32 [32, 1024, 1024], P('own', 'dp'), as said below
- root_left: bfloat16 [32, 1024, 1024], P('own', 'dp'), as said below
- root_right: bfloat16 [32, 1024, 1024], P('own', 'dp'), as said below
- master: float32 [32, 1024, 1024], P('own', 'dp'), may hold values from -4 to 4
- moment_first: float32 [32, 1024, 1024], P('own', 'dp'), may hold values from -0.6 to 0.6
- moment_second: float32 [32, 1024, 1024], P('own', 'dp'), may hold values from 0.001 to 1, as said below
Outputs:
- left_next: float32 [32, 1024, 1024], P('own', 'dp')
- right_next: float32 [32, 1024, 1024], P('own', 'dp')
- master_next: float32 [32, 1024, 1024], P('own', 'dp')
- first_next: float32 [32, 1024, 1024], P('own', 'dp')
- second_next: float32 [32, 1024, 1024], P('own', 'dp')
- weights_out: bfloat16 [16, 1024, 1024], P(None, ('dp', 'own'))
Inputs may be any that keep to these rules, and one draw needn't show every extreme that they name: `owner_map`: no two blocks share a slot. In every draw all 2 slots of some owner are taken, and so are slots 0 and 31. `root_left`: symmetric in its last two dimensions. `root_right`: symmetric in its last two dimensions. `stat_left`: symmetric in its last two dimensions. `stat_right`: symmetric in its last two dimensions. `moment_second`: Positive.
All inputs are finite; a program needn't handle non-finite values.
Results may differ from a plain program's by a relative error of at most 0.0045.
Values may be sent and summed in bfloat16 or wider, within the bound.
No kernel may reach another device: no remote copies, remote signals or barrier semaphores. Data moves between devices by JAX's collectives and lax.ppermute only.
A program may use at most 128 MiB of HBM per device.

v0:
```python
import jax
import jax.numpy as jnp
from jax import lax
from jax.sharding import PartitionSpec as P

stat_decay = 0.9
first_decay = 0.9
second_decay = 0.99
learn_rate = 0.25


def per_device(
    grads,
    owner_map,
    stat_left,
    stat_right,
    root_left,
    root_right,
    master,
    moment_first,
    moment_second,
):
    owners = lax.axis_size("own")
    slot_count = stat_left.shape[0]
    rows_dev = stat_left.shape[1]
    order_size = stat_left.shape[2]
    blocks = owner_map.shape[0]
    owned_slots = owners * slot_count
    highest = lax.Precision.HIGHEST
    matches = owner_map[:, None] == jnp.arange(owned_slots, dtype=jnp.int32)[None, :]
    occupied = jnp.any(matches, axis=0)
    block_of = jnp.sum(jnp.where(matches, jnp.arange(blocks, dtype=jnp.int32)[:, None], 0), axis=0)
    partials = grads[0]
    summed = lax.psum(partials, "dp")
    packed = jnp.where(occupied[:, None, None], jnp.take(summed, block_of, axis=0), 0.0)
    packed = packed.reshape(owners, slot_count, summed.shape[1], order_size)
    arrived = lax.all_to_all(
        packed.astype(jnp.bfloat16), "own", split_axis=0, concat_axis=2, tiled=True
    ).astype(packed.dtype)
    whole_grad = arrived.reshape(slot_count, order_size, order_size)
    first_row = lax.axis_index("dp") * rows_dev
    own_rows = lax.dynamic_slice_in_dim(whole_grad, first_row, rows_dev, 1)
    own_cols = lax.dynamic_slice_in_dim(whole_grad, first_row, rows_dev, 2)
    left_new = stat_decay * stat_left + (1.0 - stat_decay) * jnp.einsum(
        "srk,snk->srn", own_rows, whole_grad, precision=highest, preferred_element_type=jnp.float32
    )
    right_new = stat_decay * stat_right + (1.0 - stat_decay) * jnp.einsum(
        "skr,skn->srn", own_cols, whole_grad, precision=highest, preferred_element_type=jnp.float32
    )
    first_new = first_decay * moment_first + (1.0 - first_decay) * own_rows
    second_new = second_decay * moment_second + (1.0 - second_decay) * own_rows * own_rows
    adam_step = first_new / (jnp.sqrt(second_new) + 1e-08)
    rounded = whole_grad.astype(jnp.bfloat16)
    partial_product = jnp.einsum(
        "skn,srn->skr", rounded, root_right, preferred_element_type=jnp.float32
    ).astype(jnp.bfloat16)
    direction = jnp.einsum(
        "srk,skn->srn",
        root_left,
        lax.all_gather(partial_product, "dp", axis=2, tiled=True),
        preferred_element_type=jnp.float32,
    )
    square_sums = lax.psum(
        (jnp.sum(adam_step * adam_step, axis=(1, 2)), jnp.sum(direction * direction, axis=(1, 2))),
        "dp",
    )
    graft = jnp.sqrt(square_sums[0]) / (jnp.sqrt(square_sums[1]) + 1e-06)
    master_new = master - learn_rate * graft[:, None, None] * direction
    occupied_mine = lax.dynamic_slice_in_dim(
        occupied, lax.axis_index("own") * slot_count, slot_count
    )[:, None, None]
    left_next = jnp.where(occupied_mine, left_new, stat_left)
    right_next = jnp.where(occupied_mine, right_new, stat_right)
    master_next = jnp.where(occupied_mine, master_new, master)
    first_next = jnp.where(occupied_mine, first_new, moment_first)
    second_next = jnp.where(occupied_mine, second_new, moment_second)
    shares = master_new.astype(jnp.bfloat16).reshape(
        slot_count, owners, rows_dev // owners, order_size
    )
    delivered = lax.all_to_all(shares, "own", split_axis=1, concat_axis=0, tiled=True)
    delivered = delivered.reshape(owned_slots, rows_dev // owners, order_size)
    weights_out = jnp.take(delivered, owner_map, axis=0)
    return (left_next, right_next, master_next, first_next, second_next, weights_out)


def solution(mesh):
    return jax.shard_map(
        per_device,
        mesh=mesh,
        in_specs=(
            P("dp", None, "own", None),
            P(),
            P("own", "dp", None),
            P("own", "dp", None),
            P("own", "dp", None),
            P("own", "dp", None),
            P("own", "dp", None),
            P("own", "dp", None),
            P("own", "dp", None),
        ),
        out_specs=(
            P("own", "dp", None),
            P("own", "dp", None),
            P("own", "dp", None),
            P("own", "dp", None),
            P("own", "dp", None),
            P(None, ("dp", "own"), None),
        ),
        check_vma=False,
    )
```

profile of v0, /device:TPU:1, one launch (start us, length us, event | category | flops | bytes accessed | tf_op | source)
XLA Modules:
  0.0 420.0 jit_solution(211106581229123987)
XLA Ops:
  7.2 0.0 copy-start
  7.2 0.0 all-gather.2.cloned.1.call-start
  7.2 0.8 fusion.13
  8.0 0.7 select_reduce_fusion
  8.8 0.1 reduce_sum.32
  8.8 0.1 broadcast_in_dim.75
  9.0 179.9 %all-reduce.2 = bf16[16,64,1024]{2,1,0:T(8,128)(2,1)S(1)} all-reduce(f32[16,64,1024]{2,1,0:T(8,128)} %bitcast.52), channel_id=1, replica_groups=mesh['dp'=16,'own'=16] {'dp'}, use_global_device_ids=true, to_apply=%region_2.3 | all-reduce | flops 1048576 | bytes 6291456 | tf_op jit(solution)/shard_map/psum | solution.py:34
  188.9 2.8 gather_fusion
  191.6 4.3 %select_convert_fusion = bf16[16,2,64,1024]{3,2,1,0:T(8,128)(2,1)S(1)} fusion(bf16[16,2,64,1024]{3,2,1,0:T(8,128)(2,1)} %bitcast.51, pred[16,2]{1,0:T(8,128)(4,1)S(1)} %compare_and_fusion, pred[16,2]{1,0:T(8,128)(4,1)S(1)} %broadcast_in_dim.75), kind=kLoop, calls=%fused_computation.2 | loop fusion | flops 4194304 | bytes 8388672 | tf_op jit(solution)/shard_map/convert_element_type | solution.py:38
  195.9 61.4 %all_to_all.30 = bf16[16,2,64,1024]{3,2,1,0:T(8,128)(2,1)S(1)} all-to-all(bf16[16,2,64,1024]{3,2,1,0:T(8,128)(2,1)S(1)} %select_convert_fusion), channel_id=1, replica_groups=mesh['dp'=16,'own'=16] {'own'}, dimensions={0} | all-to-all | bytes 8388608 | tf_op jit(solution)/shard_map/all_to_all | solution.py:37
  257.4 0.7 copy.30
  258.1 0.0 copy-start.8
  258.1 0.0 copy-start.3
  258.1 0.0 copy-start.4
  258.1 0.0 copy-start.5
  258.1 1.9 copy-done.1
  260.1 2.1 convolution_convert_fusion
  262.2 0.0 all-gather.2.cloned.1.call-update
  262.2 0.1 dynamic_slice.13
  262.3 2.4 fusion.7
  264.8 4.5 %fusion.3 = f32[2,64,1024]{2,1,0:T(8,128)} fusion(f32[2,64,1024]{2,1,0:T(8,128)S(1)} %copy-done.5, bf16[2,1024,1024]{2,1,0:T(8,128)(2,1)} %bitcast.49, s32[]{:T(128)S(6)} %select_n.69, pred[2]{0:T(512)(128)(4,1)S(1)} %dynamic_slice.13), kind=kOutput, calls=%fused_computation.8 | convolution fusion | flops 268959744 | bytes 5505030 | tf_op jit(solution)/shard_map/srk,snk->srn/dot_general | solution.py:44
  269.3 86.4 %all-gather.2.cloned.1.call-done = bf16[2,1024,1024]{1,2,0:T(8,128)(2,1)} async-done(((bf16[2,1024,64]{1,2,0:T(8,128)(2,1)}), bf16[2,1024,1024]{1,2,0:T(8,128)(2,1)}) %all-gather.2.cloned.1.call-update) | async-done | bytes 4194320 | tf_op jit(solution)/shard_map/all_gather | solution.py:60
  355.7 3.7 multiply_reduce_fusion
  359.4 26.4 %all-reduce = (f32[2]{0:T(128)S(1)}, f32[2]{0:T(128)S(1)}) all-reduce(f32[2]{0:T(128)S(1)} %get-tuple-element.13, f32[2]{0:T(128)S(1)} %get-tuple-element.9), channel_id=1, replica_groups=mesh['dp'=16,'own'=16] {'dp'}, use_global_device_ids=true, to_apply=%region_6.7 | all-reduce | flops 4 | bytes 32 | tf_op jit(solution)/shard_map/psum | solution.py:63
  385.8 1.0 fusion.10
  386.8 0.1 reshape.74
  386.9 0.8 copy.32
  387.7 15.3 %all-to-all-start.1 = ((bf16[2,16,4,1024]{3,2,0,1:T(4,128)(2,1)}), bf16[2,16,4,1024]{3,2,0,1:T(4,128)(2,1)S(1)}, u32[]{:S(2)}, u32[]{:S(2)}) async-start(bf16[2,16,4,1024]{3,2,0,1:T(4,128)(2,1)} %copy.32), calls=%async_computation.1 | async-start | bytes 524288 | tf_op jit(solution)/shard_map/all_to_all | solution.py:80
  403.0 4.3 %fusion.1 = f32[2,64,1024]{2,1,0:T(8,128)} fusion(f32[2,64,1024]{2,1,0:T(8,128)S(1)} %copy-done.2, bf16[2,1024,1024]{2,1,0:T(8,128)(2,1)} %bitcast.50, s32[]{:T(128)S(6)} %select_n.69, pred[2]{0:T(512)(128)(4,1)S(1)} %dynamic_slice.13), kind=kOutput, calls=%fused_computation.5 | convolution fusion | flops 268959744 | bytes 5767174 | tf_op jit(solution)/shard_map/skr,skn->srn/dot_general | solution.py:47
  407.3 4.4 %all-to-all-done.1 = bf16[2,16,4,1024]{3,2,0,1:T(4,128)(2,1)S(1)} async-done(((bf16[2,16,4,1024]{3,2,0,1:T(4,128)(2,1)}), bf16[2,16,4,1024]{3,2,0,1:T(4,128)(2,1)S(1)}, u32[]{:S(2)}, u32[]{:S(2)}) %all-to-all-start.1) | async-done | bytes 262176 | tf_op jit(solution)/shard_map/all_to_all | solution.py:80
  411.7 0.7 gather_fusion.1
  412.4 0.8 broadcast_select_fusion
  (19 shorter events, 0.1 us)
Async XLA Ops:
  7.2 348.5 %copy-start = (bf16[2,64,1024]{2,1,0:T(8,128)(2,1)S(1)}, bf16[2,64,1024]{2,1,0:T(8,128)(2,1)}, u32[]{:S(2)}) copy-start(bf16[2,64,1024]{2,1,0:T(8,128)(2,1)} %param.13) | copy-start | bytes 786436
  7.2 348.5 %all-gather.2.cloned.1.call-start = ((), (), s32[]{:S(2)}) async-start(), calls=%async_computation.2 | async-start | bytes 4456448 | tf_op jit(solution)/shard_map/all_gather | solution.py:60
  257.4 2.7 copy-start.7
  258.1 2.0 copy-start.1
  258.1 4.2 copy-start.8
  258.1 4.2 %copy-start.3 = (f32[2,64,1024]{2,1,0:T(8,128)S(1)}, f32[2,64,1024]{2,1,0:T(8,128)}, u32[]{:S(2)}) copy-start(f32[2,64,1024]{2,1,0:T(8,128)} %param.17) | copy-start | bytes 1572868
  258.1 4.2 %copy-start.4 = (f32[2,64,1024]{2,1,0:T(8,128)S(1)}, f32[2,64,1024]{2,1,0:T(8,128)}, u32[]{:S(2)}) copy-start(f32[2,64,1024]{2,1,0:T(8,128)} %param.16) | copy-start | bytes 1572868
  258.1 6.6 %copy-start.5 = (f32[2,64,1024]{2,1,0:T(8,128)S(1)}, f32[2,64,1024]{2,1,0:T(8,128)}, u32[]{:S(2)}) copy-start(f32[2,64,1024]{2,1,0:T(8,128)} %param.11) | copy-start | bytes 1572868
  264.8 121.1 %copy-start.6 = (f32[2,64,1024]{2,1,0:T(8,128)S(1)}, f32[2,64,1024]{2,1,0:T(8,128)}, u32[]{:S(2)}) copy-start(f32[2,64,1024]{2,1,0:T(8,128)} %param.15) | copy-start | bytes 1572868
  269.3 133.7 %copy-start.2 = (f32[2,64,1024]{2,1,0:T(8,128)S(1)}, f32[2,64,1024]{2,1,0:T(8,128)}, u32[]{:S(2)}) copy-start(f32[2,64,1024]{2,1,0:T(8,128)} %param.12) | copy-start | bytes 1572868
  387.7 24.0 %all-to-all-start.1 = ((bf16[2,16,4,1024]{3,2,0,1:T(4,128)(2,1)}), bf16[2,16,4,1024]{3,2,0,1:T(4,128)(2,1)S(1)}, u32[]{:S(2)}, u32[]{:S(2)}) async-start(bf16[2,16,4,1024]{3,2,0,1:T(4,128)(2,1)} %copy.32), calls=%async_computation.1 | async-start | bytes 524288 | tf_op jit(solution)/shard_map/all_to_all | solution.py:80
Sparse Core Ops, SparseCore 0:
  262.3 93.3 all-gather.1
where the time goes:
time: 420 us
  blocking collectives  268 us (64%)
  waiting for transfers between devices  90.8 us (22%)
  starting transfers between devices  15.3 us (4%)
  matrix products  14.6 us (3%)
  between operations  14.2 us (3%)
  other arithmetic  10.1 us (2%)
  local copies, waits for them, and re-layouts  7.27 us (2%)
    psum x1, blocking collectives, per_device(): summed = lax.psum(partials, 'dp')  180 us
    all_gather x1, waiting for transfers between devices, per_device(): lax.all_gather(partial_product, 'dp', axis=2, tiled=True)  86.4 us
    all_to_all x1, blocking collectives, per_device(): lax.all_to_all(packed.astype(jnp.bfloat16), 'own', split_axis=0, concat_a...  61.4 us
    psum x1, blocking collectives, per_device(): lax.psum((jnp.sum(adam_step * adam_step, axis=(1, 2)), jnp.sum(direction...  26.4 us
    all_to_all x1, starting transfers between devices, per_device(): lax.all_to_all(shares, 'own', split_axis=1, concat_axis=0, tiled=True)  15.3 us
  transfers between devices with their start and end apart: 2, of which 2 were waited for; matrix products, arithmetic and copies ran while one was open for 3% of the time, Pallas kernels for 0%

commit v1 on v0

--- a/solution.py
+++ b/solution.py
@@ -31,7 +31,7 @@
     occupied = jnp.any(matches, axis=0)
     block_of = jnp.sum(jnp.where(matches, jnp.arange(blocks, dtype=jnp.int32)[:, None], 0), axis=0)
     partials = grads[0]
-    summed = lax.psum(partials, "dp")
+    summed = jnp.sum(lax.all_gather(partials, "dp"), axis=0)
     packed = jnp.where(occupied[:, None, None], jnp.take(summed, block_of, axis=0), 0.0)
     packed = packed.reshape(owners, slot_count, summed.shape[1], order_size)
     arrived = lax.all_to_all(

time: 420 us -> 1630 us (3.88)
  waiting for transfers between devices: 90.8 us -> 1460 us
  blocking collectives: 268 us -> 84 us
  other arithmetic: 10.1 us -> 33.3 us
    all_gather x0 -> x1, waiting for transfers between devices: none -> 1370 us  [per_device(): summed = jnp.sum(lax.all_gather(partials, 'dp'), axis=0)]
    psum x1 -> x0, blocking collectives: 180 us -> none  [per_device(): summed = lax.psum(partials, 'dp')]
    reduce_sum x0 -> x1, other arithmetic: none -> 21.2 us  [per_device(): summed = jnp.sum(lax.all_gather(partials, 'dp'), axis=0)]
  transfers between devices with their start and end apart: 2 -> 3, of which waited for: 2 -> 3; matrix products, arithmetic and copies ran while one was open for 3% -> 1% of each run, Pallas kernels for 0% -> 0%
where the time goes in v1:
time: 1630 us
  waiting for transfers between devices  1460 us (90%)
  blocking collectives  84 us (5%)
  other arithmetic  33.3 us (2%)
    all_gather x1, waiting for transfers between devices, per_device(): summed = jnp.sum(lax.all_gather(partials, 'dp'), axis=0)  1370 us
    all_gather x1, waiting for transfers between devices, per_device(): lax.all_gather(partial_product, 'dp', axis=2, tiled=True)  84.7 us
    all_to_all x1, blocking collectives, per_device(): lax.all_to_all(packed.astype(jnp.bfloat16), 'own', split_axis=0, concat_a...  57.5 us
  transfers between devices with their start and end apart: 3, of which 3 were waited for; matrix products, arithmetic and copies ran while one was open for 1% of the time, Pallas kernels for 0%

profile of v1, /device:TPU:1, one launch (start us, length us, event | category | flops | bytes accessed | tf_op | source)
XLA Modules:
  0.0 1627.0 jit_solution(7457405055018599817)
XLA Ops:
  7.2 0.0 all-gather.3.cloned.1.call-start
  7.2 0.7 all-gather.3.cloned.1.call-update
  7.9 0.0 all-gather.5.cloned.1.call-start
  8.0 0.1 select_reduce_fusion
  8.1 0.1 reduce_sum.41
  8.2 0.1 fusion.12
  8.2 0.1 broadcast_in_dim.75
  8.4 1367.2 %all-gather.3.cloned.1.call-done = f32[16,16,64,1024]{3,2,1,0:T(8,128)} async-done(((f32[1,16,64,1024]{3,2,1,0:T(8,128)}), f32[16,16,64,1024]{3,2,1,0:T(8,128)}) %all-gather.3.cloned.1.call-update) | async-done | bytes 67108880 | tf_op jit(solution)/shard_map/all_gather | solution.py:34
  1375.6 21.2 %reduce_sum.42 = bf16[16,64,1024]{2,1,0:T(8,128)(2,1)S(1)} reduce(f32[16,16,64,1024]{3,2,1,0:T(8,128)} %all-gather.3.cloned.1.call-done, f32[]{:T(128)} %constant.30.clone.1), dimensions={0}, to_apply=%region_2.3 | reduce | flops 15728640 | bytes 69206016 | tf_op jit(solution)/shard_map/reduce_sum | solution.py:34
  1396.8 2.8 gather_fusion
  1399.5 4.3 select_convert_fusion
  1403.8 57.5 %all_to_all.30 = bf16[16,2,64,1024]{3,2,1,0:T(8,128)(2,1)S(1)} all-to-all(bf16[16,2,64,1024]{3,2,1,0:T(8,128)(2,1)S(1)} %select_convert_fusion), channel_id=1, replica_groups=mesh['dp'=16,'own'=16] {'own'}, dimensions={0} | all-to-all | bytes 8388608 | tf_op jit(solution)/shard_map/all_to_all | solution.py:37
  1461.4 0.7 copy.29
  1462.1 1.5 copy-done.3
  1463.6 1.9 copy-done.1
  1465.5 2.1 convolution_convert_fusion
  1467.7 0.1 dynamic_slice.13
  1467.8 3.2 bitcast_convert_fusion
  1471.1 1.7 copy.31
  1472.7 2.6 fusion.10
  1475.3 2.2 fusion.3
  1477.5 84.7 %all-gather.5.cloned.1.call-done = bf16[2,1024,1024]{1,2,0:T(8,128)(2,1)} async-done(((bf16[2,1024,64]{1,2,0:T(8,128)(2,1)}), bf16[2,1024,1024]{1,2,0:T(8,128)(2,1)}) %all-gather.5.cloned.1.call-update) | async-done | bytes 4194320 | tf_op jit(solution)/shard_map/all_gather | solution.py:60
  1562.2 3.7 multiply_reduce_fusion
  1565.9 26.5 %all-reduce = (f32[2]{0:T(128)S(1)}, f32[2]{0:T(128)S(1)}) all-reduce(f32[2]{0:T(128)S(1)} %get-tuple-element.13, f32[2]{0:T(128)S(1)} %get-tuple-element.9), channel_id=1, replica_groups=mesh['dp'=16,'own'=16] {'dp'}, use_global_device_ids=true, to_apply=%region_6.7 | all-reduce | flops 4 | bytes 32 | tf_op jit(solution)/shard_map/psum | solution.py:63
  1592.4 1.0 fusion.7
  1593.4 0.1 reshape.74
  1593.5 0.8 copy.32
  1594.3 15.7 all-to-all-start.1
  1610.0 4.3 fusion.1
  1614.3 4.4 all-to-all-done.1
  1618.7 0.7 gather_fusion.1
  1619.4 0.8 broadcast_select_fusion
  (26 shorter events, 0.1 us)
Async XLA Ops:
  7.2 1555.1 %copy-start = (bf16[2,64,1024]{2,1,0:T(8,128)(2,1)S(1)}, bf16[2,64,1024]{2,1,0:T(8,128)(2,1)}, u32[]{:S(2)}) copy-start(bf16[2,64,1024]{2,1,0:T(8,128)(2,1)} %param.13) | copy-start | bytes 786436
  7.2 0.8 copy-start.9
  7.2 1368.4 %all-gather.3.cloned.1.call-start = ((), (), s32[]{:S(2)}) async-start(), calls=%async_computation.2 | async-start | bytes 71303168 | tf_op jit(solution)/shard_map/all_gather | solution.py:34
  7.9 1554.3 %all-gather.5.cloned.1.call-start = ((), (), s32[]{:S(2)}) async-start(), calls=%async_computation.3 | async-start | bytes 4456448 | tf_op jit(solution)/shard_map/all_gather | solution.py:60
  1461.4 2.2 copy-start.3
  1461.4 4.2 copy-start.8
  1463.6 1.9 copy-start.1
  1471.0 1.7 copy-start.7
  1471.0 4.3 copy-start.2
  1471.0 4.3 copy-start.5
  1475.3 117.1 %copy-start.6 = (f32[2,64,1024]{2,1,0:T(8,128)S(1)}, f32[2,64,1024]{2,1,0:T(8,128)}, u32[]{:S(2)}) copy-start(f32[2,64,1024]{2,1,0:T(8,128)} %param.15) | copy-start | bytes 1572868
  1477.5 132.5 %copy-start.4 = (f32[2,64,1024]{2,1,0:T(8,128)S(1)}, f32[2,64,1024]{2,1,0:T(8,128)}, u32[]{:S(2)}) copy-start(f32[2,64,1024]{2,1,0:T(8,128)} %param.12) | copy-start | bytes 1572868
  1594.3 24.4 %all-to-all-start.1 = ((bf16[2,16,4,1024]{3,2,0,1:T(4,128)(2,1)}), bf16[2,16,4,1024]{3,2,0,1:T(4,128)(2,1)S(1)}, u32[]{:S(2)}, u32[]{:S(2)}) async-start(bf16[2,16,4,1024]{3,2,0,1:T(4,128)(2,1)} %copy.32), calls=%async_computation.1 | async-start | bytes 524288 | tf_op jit(solution)/shard_map/all_to_all | solution.py:80
Sparse Core Ops, SparseCore 0:
  9.8 1365.7 all-gather.2
  1467.8 94.3 all-gather.4
